TPU v7x, 256 devices: a whole 4x4x8 slice. The times are simulated.
256 devices in a mesh: dp: 16 (over z, core), tensor: 16 (over y, x).
Axes of the slice: x: 4, y: 4, z: 8, core: 2. Of those that a mesh axis runs over, the one named last changes fastest.
Arguments:
- tokens: bfloat16 [2048, 8192], P(('dp', 'tensor')), may hold values from -6 to 6
- hidden_grad: bfloat16 [2048, 14336], P('dp', 'tensor'), may hold values from -1.5 to 1.5
- gate_tiles: bfloat16 [16, 208, 128, 128], P('tensor', 'dp'), may hold values from -0.125 to 0.125
- up_tiles: bfloat16 [16, 208, 128, 128], P('tensor', 'dp'), may hold values from -0.125 to 0.125
- tile_rows: int32 [2, 112, 16], P(None, 'tensor'), may hold values from 0 to 63, all different within a row
- tile_owner: int32 [2, 112, 16], P(None, 'tensor'), may hold values from 0 to 15, as said below
Outputs:
- hidden: bfloat16 [2048, 14336], P('dp', 'tensor')
- token_grad: bfloat16 [2048, 8192], P(('dp', 'tensor'))
- gate_grad: bfloat16 [16, 208, 128, 128], P('tensor', 'dp')
- up_grad: bfloat16 [16, 208, 128, 128], P('tensor', 'dp')
Inputs may be any that keep to these rules, and one draw needn't show every extreme that they name: Each row tile_rows[m, f, :] names 16 different row blocks. For each m and t, among the 112 entries tile_owner[m, t * 7 .. (t + 1) * 7 - 1, :] no owner appears more than 13 times, and some owner appears exactly 13 times.
All inputs are finite; a program needn't handle non-finite values.
Results may differ from a plain program's by a relative error of at most 0.018.
Values may be sent and summed in bfloat16 or wider, within the bound.
No kernel may reach another device: no remote copies, remote signals or barrier semaphores. Data moves between devices by JAX's collectives and lax.ppermute only.
A program may use at most 128 MiB of HBM per device.

v0:
```python
import jax
import jax.numpy as jnp
from jax import lax
from jax.sharding import PartitionSpec as P


def slot_index(owner_ids, capacity):
    tile_total = owner_ids.shape[0]
    tile_order = jnp.arange(tile_total, dtype=jnp.int32)
    same_owner = (owner_ids[:, None] == owner_ids[None, :]) & (
        tile_order[None, :] < tile_order[:, None]
    )
    tile_ranks = jnp.sum(same_owner.astype(jnp.int32), axis=1)
    return owner_ids * capacity + tile_ranks


def body(tokens, hidden_grad, gate_tiles, up_tiles, tile_rows, tile_owner):
    tile_size = gate_tiles.shape[2]
    capacity = gate_tiles.shape[1]
    owner_count = lax.axis_size("dp")
    slot_total = capacity * owner_count
    gathered_tok = lax.all_gather(tokens, "tensor", axis=0, tiled=True)
    tok_count, model_width = gathered_tok.shape
    row_blocks = model_width // tile_size
    tok_blocks = gathered_tok.reshape(tok_count, row_blocks, tile_size)
    group_blocks = tile_rows.shape[1]
    per_block = tile_rows.shape[2]
    tile_count = group_blocks * per_block
    block_ids = jnp.arange(tile_count, dtype=jnp.int32) // per_block
    row_flat = tile_rows.reshape(2, tile_count)
    slot_stack = jnp.stack(
        [
            slot_index(tile_owner[0].reshape(-1), capacity),
            slot_index(tile_owner[1].reshape(-1), capacity),
        ],
        axis=0,
    )
    slot_grid = jnp.arange(slot_total, dtype=jnp.int32)
    slot_match = (slot_stack[:, None, :] == slot_grid[None, :, None]).astype(jnp.int32)
    slot_live = jnp.sum(slot_match, axis=2)
    slot_row = jnp.sum(slot_match * row_flat[:, None, :], axis=2)
    slot_block = jnp.sum(slot_match * block_ids[None, None, :], axis=2)
    slot_target = jnp.where(slot_live == 1, slot_block, group_blocks)
    local_gate = gate_tiles[0]
    local_up = up_tiles[0]
    gate_store, up_store = (
        lax.all_gather(local_gate, "dp", axis=0, tiled=True),
        lax.all_gather(local_up, "dp", axis=0, tiled=True),
    )
    gate_panel = jnp.take(gate_store, slot_stack[0], axis=0).reshape(
        group_blocks, per_block, tile_size, tile_size
    )
    up_panel = jnp.take(up_store, slot_stack[1], axis=0).reshape(
        group_blocks, per_block, tile_size, tile_size
    )
    picked = jnp.take(tok_blocks, row_flat.reshape(-1), axis=1).reshape(
        tok_count, 2, group_blocks, per_block, tile_size
    )
    gate_pre = jnp.einsum(
        "nfkr,fkrc->nfc", picked[:, 0], gate_panel, preferred_element_type=jnp.float32
    ).reshape(tok_count, group_blocks * tile_size)
    up_pre = jnp.einsum(
        "nfkr,fkrc->nfc", picked[:, 1], up_panel, preferred_element_type=jnp.float32
    ).reshape(tok_count, group_blocks * tile_size)
    hidden = (jax.nn.silu(gate_pre) * up_pre).astype(jnp.bfloat16)
    gate_sig = jax.nn.sigmoid(gate_pre)
    delta_full = hidden_grad.astype(jnp.float32)
    gate_delta = (delta_full * up_pre * gate_sig * (1.0 + gate_pre * (1.0 - gate_sig))).astype(
        jnp.bfloat16
    )
    up_delta = (delta_full * gate_pre * gate_sig).astype(jnp.bfloat16)
    delta_stack = jnp.stack(
        [
            gate_delta.reshape(tok_count, group_blocks, tile_size),
            up_delta.reshape(tok_count, group_blocks, tile_size),
        ],
        axis=1,
    )
    panel_stack = jnp.stack([gate_panel, up_panel], axis=0)
    back_rows = jnp.einsum(
        "nmfc,mfkrc->mfknr", delta_stack, panel_stack, preferred_element_type=jnp.float32
    )
    back_flat = back_rows.reshape(2 * tile_count, tok_count, tile_size)
    row_sums = jax.ops.segment_sum(back_flat, row_flat.reshape(-1), num_segments=row_blocks)
    token_part = row_sums.transpose(1, 0, 2).reshape(tok_count, model_width)
    token_grad = lax.psum_scatter(
        token_part.astype(jnp.bfloat16), "tensor", scatter_dimension=0, tiled=True
    )
    zero_block = jnp.zeros((tok_count, 2, 1, tile_size), jnp.bfloat16)
    delta_padded = jnp.concatenate([delta_stack, zero_block], axis=2).reshape(
        tok_count, 2 * (group_blocks + 1), tile_size
    )
    matrix_base = jnp.arange(2, dtype=jnp.int32) * (group_blocks + 1)
    target_part = slot_target + matrix_base[:, None]
    chosen = jnp.take(tok_blocks, slot_row.reshape(-1), axis=1).reshape(
        tok_count, 2, capacity * lax.axis_size("dp"), tile_size
    )
    delta_part = jnp.take(delta_padded, target_part.reshape(-1), axis=1).reshape(
        tok_count, 2, capacity * lax.axis_size("dp"), tile_size
    )
    tile_sums = lax.psum_scatter(
        jnp.einsum(
            "nmsr,nmsc->smrc", chosen, delta_part, preferred_element_type=jnp.float32
        ).astype(jnp.bfloat16),
        "dp",
        scatter_dimension=0,
        tiled=True,
    ).astype(jnp.float32)
    gate_grad = tile_sums[:, 0].astype(jnp.bfloat16)[None]
    up_grad = tile_sums[:, 1].astype(jnp.bfloat16)[None]
    return (hidden, token_grad, gate_grad, up_grad)


def solution(mesh):
    placed = (
        P(("dp", "tensor"), None),
        P("dp", "tensor"),
        P("tensor", "dp", None, None),
        P("tensor", "dp", None, None),
        P(None, "tensor", None),
        P(None, "tensor", None),
    )
    return jax.shard_map(
        body,
        mesh=mesh,
        in_specs=placed,
        out_specs=(
            P("dp", "tensor"),
            P(("dp", "tensor"), None),
            P("tensor", "dp", None, None),
            P("tensor", "dp", None, None),
        ),
        check_vma=False,
    )
```

profile of v0, /device:TPU:2, one launch (start us, length us, event | category | flops | bytes accessed | tf_op | source)
XLA Modules:
  0.0 453.2 jit_solution(11754717820026690466)
XLA Ops:
  7.2 0.7 all-gather.6.cloned.1.call-update
  7.9 0.7 all-gather.10.cloned.1.call-update
  8.7 0.7 all-gather.8.cloned.1.call-update
  9.4 0.7 copy.79
  10.4 0.7 compare_and_fusion
  11.1 0.8 multiply_reduce_fusion.1
  12.2 0.2 convert_reduce_fusion.1
  12.4 0.2 convert_reduce_fusion.2
  12.6 0.3 select_reduce_fusion.1
  12.9 0.1 reshape.263
  13.2 1.1 copy.85
  14.4 48.5 %all-gather.6.cloned.1.call-done = bf16[128,8192]{1,0:T(8,128)(2,1)} async-done(((bf16[8,8192]{1,0:T(8,128)(2,1)}), bf16[128,8192]{1,0:T(8,128)(2,1)}) %all-gather.6.cloned.1.call-update) | async-done | bytes 2097168 | tf_op jit(solution)/shard_map/all_gather | solution.py:22
  63.0 4.1 copy.78
  67.1 3.2 copy.80
  70.3 8.3 %gather_fusion = bf16[224,128,128]{2,1,0:T(8,128)(2,1)} fusion(bf16[128,64,128]{2,0,1:T(8,128)(2,1)S(1)} %copy.80, s32[1024]{0:T(1024)S(1)} %pad_clamp_fusion.3), kind=kCustom, calls=%fused_computation.2 | custom fusion | bytes 14680960 | tf_op jit(solution)/shard_map/jit(_take)/gather | solution.py:56
  78.6 12.8 %gather_fusion.1 = bf16[416,128,128]{2,1,0:T(8,128)(2,1)} fusion(bf16[128,64,128]{2,0,1:T(8,128)(2,1)S(1)} %copy.80, s32[1024]{0:T(1024)S(1)} %pad_clamp_fusion.1), kind=kCustom, calls=%fused_computation.3 | custom fusion | bytes 27264640 | tf_op jit(solution)/shard_map/jit(_take)/gather | solution.py:95
  91.5 12.9 %copy.92 = bf16[128,416,128]{2,1,0:T(8,128)(2,1)} copy(bf16[128,416,128]{2,0,1:T(8,128)(2,1)} %bitcast.94) | data formatting | bytes 27262976 | tf_op jit(solution)/shard_map/jit(_take)/gather | solution.py:95
  104.3 3.7 broadcast_select_fusion.2
  108.0 11.5 %broadcast_select_fusion.1 = bf16[128,2,208,128]{3,2,1,0:T(8,128)(2,1)} fusion(bf16[128,2,208,128]{3,2,1,0:T(8,128)(2,1)} %bitcast.92, pred[2,208]{1,0:T(4,128)(4,1)S(1)} %compare_and_fusion.2), kind=kLoop, calls=%fused_computation.10 | loop fusion | flops 6815744 | bytes 27263392 | tf_op jit(solution)/shard_map/jit(_take)/select_n | solution.py:95
  119.5 5.9 %gather_fusion.4 = bf16[112,128,128]{2,1,0:T(8,128)(2,1)} fusion(bf16[208,128,128]{2,1,0:T(8,128)(2,1)} %bitcast.105, s32[1024]{0:T(1024)S(1)} %pad_clamp_fusion.2), kind=kCustom, calls=%fused_computation.1.clone | custom fusion | bytes 7340480 | tf_op jit(solution)/shard_map/jit(_take)/gather | solution.py:53
  125.4 4.3 broadcast_select_fusion.3
  129.8 32.2 %all-gather.8.cloned.1.call-done = bf16[1,208,128,128]{3,2,0,1:T(8,128)(2,1)} async-done(((bf16[1,13,128,128]{3,2,0,1:T(8,128)(2,1)}), bf16[1,208,128,128]{3,2,0,1:T(8,128)(2,1)}) %all-gather.8.cloned.1.call-update) | async-done | bytes 6815760 | tf_op jit(solution)/shard_map/all_gather | solution.py:47
  161.9 6.0 %gather_fusion.3 = bf16[112,128,128]{2,1,0:T(8,128)(2,1)} fusion(bf16[208,128,128]{2,1,0:T(8,128)(2,1)} %bitcast.106, s32[1024]{0:T(1024)S(1)} %pad_clamp_fusion.4), kind=kCustom, calls=%fused_computation.clone | custom fusion | bytes 7340480 | tf_op jit(solution)/shard_map/jit(_take)/gather | solution.py:50
  167.9 2.6 broadcast_select_fusion.4
  170.5 0.5 copy-done.1
  171.0 5.0 %fusion.12 = f32[7,128,128,1]{2,1,3,0:T(8,128)S(1)} fusion(bf16[7,16,128,128]{3,2,1,0:T(8,128)(2,1)S(1)} %bitcast.98, bf16[128,2,7,16,128]{4,0,3,2,1:T(8,128)(2,1)} %broadcast_select_fusion.2), kind=kOutput, calls=%fused_computation.18 | convolution fusion | flops 469762048 | bytes 7798784 | tf_op jit(solution)/shard_map/nfkr,fkrc->nfc/dot_general | solution.py:62
  176.0 1.3 fusion.13
  177.3 0.3 fusion.16
  177.6 0.2 copy.86
  177.8 0.2 copy.87
  178.0 10.5 %fusion.8 = f32[2,7,16,128,128]{4,3,2,1,0:T(8,128)} fusion(bf16[1,7,16,128,128]{4,3,2,1,0:T(8,128)(2,1)} %bitcast.97, bf16[1,7,16,128,128]{4,3,2,1,0:T(8,128)(2,1)} %bitcast.100, bf16[128,1,7,128]{3,0,2,1:T(8,128)(2,1)S(1)} %copy.87, bf16[128,1,7,128]{3,0,2,1:T(8,128)(2,1)S(1)} %copy.86), kind=kOutput, calls=%fused_computation.12 | convolution fusion | flops 943423488 | bytes 22478848 | tf_op jit(solution)/shard_map/nmfc,mfkrc->mfknr/dot_general | solution.py:80
  188.6 15.2 %copy.88 = f32[224,128,128]{2,1,0:T(8,128)} copy(f32[224,128,128]{1,2,0:T(8,128)} %bitcast.91) | data formatting | bytes 29360128 | tf_op jit(solution)/shard_map/reshape | solution.py:83
  203.7 2.5 broadcast_in_dim.57
  206.2 46.3 %scatter_fusion = f32[64,128,128]{2,1,0:T(8,128)} fusion(f32[64,128,128]{2,1,0:T(8,128)} %broadcast_in_dim.57, s32[224]{0:T(256)S(1)} %reshape.307, f32[224,128,128]{2,1,0:T(8,128)} %copy.88), kind=kCustom, calls=%fused_computation.5 | custom fusion | flops 3670016 | bytes 44041088 | tf_op jit(solution)/shard_map/scatter-add | solution.py:84
  252.5 2.6 convert_bitcast_fusion
  255.0 3.0 copy.89
  258.1 12.8 %gather_fusion.2 = bf16[416,128,128]{2,1,0:T(8,128)(2,1)} fusion(bf16[128,16,128]{2,0,1:T(8,128)(2,1)S(1)} %bitcast.90, s32[1024]{0:T(1024)S(1)} %pad_clamp_fusion), kind=kCustom, calls=%fused_computation.4 | custom fusion | bytes 27264640 | tf_op jit(solution)/shard_map/jit(_take)/gather | solution.py:98
  270.9 13.1 %copy.93 = bf16[128,416,128]{2,1,0:T(8,128)(2,1)S(1)} copy(bf16[128,416,128]{2,0,1:T(8,128)(2,1)} %bitcast.95) | data formatting | bytes 27262976 | tf_op jit(solution)/shard_map/jit(_take)/gather | solution.py:98
  284.1 5.8 %broadcast_select_fusion = bf16[128,2,208,128]{3,2,1,0:T(8,128)(2,1)} fusion(bf16[128,2,208,128]{3,2,1,0:T(8,128)(2,1)S(1)} %bitcast.93, pred[2,208]{1,0:T(4,128)(4,1)S(1)} %get-tuple-element.28), kind=kLoop, calls=%fused_computation.9 | loop fusion | flops 6815744 | bytes 27263392 | tf_op jit(solution)/shard_map/jit(_take)/select_n | solution.py:98
  289.8 37.8 %fusion.3 = bf16[208,2,128,128]{3,2,1,0:T(8,128)(2,1)} fusion(bf16[128,2,208,128]{3,2,1,0:T(8,128)(2,1)} %broadcast_select_fusion, bf16[128,2,208,128]{3,2,1,0:T(8,128)(2,1)} %broadcast_select_fusion.1), kind=kOutput, calls=%fused_computation.11 | convolution fusion | flops 1751646208 | bytes 40894464 | tf_op jit(solution)/shard_map/nmsr,nmsc->smrc/dot_general | solution.py:102
  327.6 0.6 copy-done.3
  328.3 0.6 dynamic-slice
  329.5 0.8 copy.96
  330.4 27.2 %all-reduce.4.cloned.1.call-done = bf16[128,8192]{0,1:T(8,128)(2,1)} async-done(((bf16[128,8192]{0,1:T(8,128)(2,1)}), bf16[128,8192]{0,1:T(8,128)(2,1)}) %all-reduce.4.cloned.1.call-update) | async-done | bytes 2097168
  357.6 2.2 constant_dynamic-slice_fusion
  359.8 1.4 copy.97
  361.2 83.3 %reduce-scatter.3.cloned.1.call-done = bf16[13,2,128,128]{3,2,1,0:T(8,128)(2,1)} async-done(((bf16[208,2,128,128]{3,2,1,0:T(8,128)(2,1)}), bf16[13,2,128,128]{3,2,1,0:T(8,128)(2,1)}) %reduce-scatter.3.cloned.1.call-update) | async-done | bytes 851984 | tf_op jit(solution)/shard_map/reduce_scatter | solution.py:101
  444.5 2.1 slice_bitcast_fusion.4
  (46 shorter events, 1.2 us)
Async XLA Ops:
  7.2 55.8 %all-gather.6.cloned.1.call-start = ((), (), s32[]{:S(2)}) async-start(), calls=%async_computation.1 | async-start | bytes 2228224 | tf_op jit(solution)/shard_map/all_gather | solution.py:22
  7.9 111.6 %all-gather.10.cloned.1.call-start = ((), (), s32[]{:S(2)}) async-start(), calls=%async_computation.4 | async-start | bytes 7241728 | tf_op jit(solution)/shard_map/all_gather | solution.py:48
  8.6 153.3 %all-gather.8.cloned.1.call-start = ((), (), s32[]{:S(2)}) async-start(), calls=%async_computation.3 | async-start | bytes 7241728 | tf_op jit(solution)/shard_map/all_gather | solution.py:47
  9.4 348.2 %all-reduce.4.cloned.1.call-start = ((), (), s32[]{:S(2)}) async-start(), calls=%async_computation.5 | async-start | bytes 4194304
  91.5 12.9 %copy-start = (bf16[224,128,128]{2,1,0:T(8,128)(2,1)S(1)}, bf16[224,128,128]{2,1,0:T(8,128)(2,1)}, u32[]{:S(2)}) copy-start(bf16[224,128,128]{2,1,0:T(8,128)(2,1)} %gather_fusion) | copy-start | bytes 22020100
  161.9 14.1 %slice-start = ((s8[7340032]{0:T(1024)(128)(4,1)}), s8[3145728]{0:T(1024)(128)(4,1)S(1)}, s32[]{:S(2)}) async-start(s8[7340032]{0:T(1024)(128)(4,1)} %bitcast.103), calls=%async_computation.6 | async-start | bytes 6291456
  167.9 3.1 copy-start.1
  167.9 8.1 %slice-start.1 = ((s8[7340032]{0:T(1024)(128)(4,1)}), s8[4194304]{0:T(1024)(128)(4,1)S(1)}, s32[]{:S(2)}) async-start(s8[7340032]{0:T(1024)(128)(4,1)} %bitcast.103), calls=%async_computation.7 | async-start | bytes 8388608
  170.5 6.8 %copy-start.2 = (bf16[112,128,128]{2,1,0:T(8,128)(2,1)}, bf16[112,128,128]{2,1,0:T(8,128)(2,1)S(1)}, u32[]{:S(2)}) copy-start(bf16[112,128,128]{2,1,0:T(8,128)(2,1)S(1)} %broadcast_select_fusion.4) | copy-start | bytes 11010052
  258.0 186.5 %reduce-scatter.3.cloned.1.call-start = ((), (), s32[]{:S(2)}) async-start(), calls=%async_computation.2 | async-start | bytes 14483456 | tf_op jit(solution)/shard_map/reduce_scatter | solution.py:101
  327.6 0.7 copy-start.3
Sparse Core Ops, SparseCore 0:
  10.4 52.5 all-gather.5
  64.8 48.1 all-gather.9
  114.8 47.0 all-gather.7
  258.1 99.4 all-reduce.3
  360.0 84.4 reduce-scatter.2
where the time goes:
time: 455 us; the launch traced here: 453 us
  waiting for transfers between devices  193 us (42%)
  local copies, waits for them, and re-layouts  111 us (24%)
  other arithmetic  79.4 us (17%)
  matrix products  54.5 us (12%)
  between operations  14.7 us (3%)
    reduce_scatter x1, waiting for transfers between devices, body(): lax.psum_scatter(jnp.einsum('nmsr,nmsc->smrc', chosen, delta_part, prefer...  83.3 us
    all_gather x1, waiting for transfers between devices, body(): gathered_tok = lax.all_gather(tokens, 'tensor', axis=0, tiled=True)  48.5 us
    scatter-add x1, other arithmetic, body(): jax.ops.segment_sum(back_flat, row_flat.reshape(-1), num_segments=row_blo...  46.3 us
    dot_general x1, matrix products, body(): jnp.einsum('nmsr,nmsc->smrc', chosen, delta_part, preferred_element_type=...  37.8 us
    all_gather x1, waiting for transfers between devices, body(): lax.all_gather(local_gate, 'dp', axis=0, tiled=True)  32.2 us
    unnamed x6, waiting for transfers between devices  29.3 us
    gather x2, local copies, waits for them, and re-layouts, body(): jnp.take(delta_padded, target_part.reshape(-1), axis=1)  25.9 us
    gather x2, local copies, waits for them, and re-layouts, body(): jnp.take(tok_blocks, slot_row.reshape(-1), axis=1)  25.7 us
  transfers between devices with their start and end apart: 5, of which 4 were waited for; matrix products, arithmetic and copies ran while one was open for 32% of the time, Pallas kernels for 0%

commit v1 on v0

--- a/solution.py
+++ b/solution.py
@@ -44,7 +44,9 @@
     local_gate = gate_tiles[0]
     local_up = up_tiles[0]
     gate_store, up_store = (
-        lax.all_gather(local_gate, "dp", axis=0, tiled=True),
+        jnp.concatenate(
+            lax.all_to_all(jnp.stack([local_gate] * lax.axis_size("dp")), "dp", 0, 0), axis=0
+        ),
         lax.all_gather(local_up, "dp", axis=0, tiled=True),
     )
     gate_panel = jnp.take(gate_store, slot_stack[0], axis=0).reshape(

time: 455 us -> 509 us (1.12)
  waiting for transfers between devices: 193 us -> 237 us
  starting transfers between devices: 0.19 us -> 8.9 us
    all_gather x1, waiting for transfers between devices: 0.01 us -> 83.8 us  [body(): lax.all_gather(local_up, 'dp', axis=0, tiled=True)]
    all_gather x1 -> x0, waiting for transfers between devices: 32.2 us -> none  [body(): lax.all_gather(local_gate, 'dp', axis=0, tiled=True)]
    all_gather x1, waiting for transfers between devices: 48.5 us -> 38.2 us  [body(): gathered_tok = lax.all_gather(tokens, 'tensor', axis=0, tiled=True)]
    all_to_all x0 -> x1, starting transfers between devices: none -> 8.75 us  [body(): lax.all_to_all(jnp.stack([local_gate] * lax.axis_size('dp')), 'dp', 0, 0)]
    another operation x0 -> x1, local copies, waits for them, and re-layouts: none -> 5.57 us  [body(): jnp.stack([local_gate] * lax.axis_size('dp'))]
    unnamed x6 -> x5, waiting for transfers between devices: 29.3 us -> 31.3 us
  transfers between devices with their start and end apart: 5 -> 5, of which waited for: 4 -> 4; matrix products, arithmetic and copies ran while one was open for 32% -> 29% of each run, Pallas kernels for 0% -> 0%
where the time goes in v1:
time: 509 us; the launch traced here: 507 us
  waiting for transfers between devices  237 us (47%)
  local copies, waits for them, and re-layouts  115 us (23%)
  other arithmetic  77.9 us (15%)
  matrix products  54.4 us (11%)
  between operations  14.7 us (3%)
  starting transfers between devices  8.9 us (2%)
    all_gather x1, waiting for transfers between devices, body(): lax.all_gather(local_up, 'dp', axis=0, tiled=True)  83.8 us
    reduce_scatter x1, waiting for transfers between devices, body(): lax.psum_scatter(jnp.einsum('nmsr,nmsc->smrc', chosen, delta_part, prefer...  83.3 us
    scatter-add x1, other arithmetic, body(): jax.ops.segment_sum(back_flat, row_flat.reshape(-1), num_segments=row_blo...  46.3 us
    all_gather x1, waiting for transfers between devices, body(): gathered_tok = lax.all_gather(tokens, 'tensor', axis=0, tiled=True)  38.2 us
    dot_general x1, matrix products, body(): jnp.einsum('nmsr,nmsc->smrc', chosen, delta_part, preferred_element_type=...  37.7 us
    unnamed x5, waiting for transfers between devices  31.3 us
    gather x2, local copies, waits for them, and re-layouts, body(): jnp.take(delta_padded, target_part.reshape(-1), axis=1)  25.9 us
    gather x2, local copies, waits for them, and re-layouts, body(): jnp.take(tok_blocks, slot_row.reshape(-1), axis=1)  25.5 us
  transfers between devices with their start and end apart: 5, of which 4 were waited for; matrix products, arithmetic and copies ran while one was open for 29% of the time, Pallas kernels for 0%

profile of v1, /device:TPU:2, one launch (start us, length us, event | category | flops | bytes accessed | tf_op | source)
XLA Modules:
  0.0 507.3 jit_solution(2182706254111732696)
XLA Ops:
  7.2 0.7 all-gather.4.cloned.1.call-update
  7.9 0.7 all-gather.6.cloned.1.call-update
  8.6 5.6 %stack.14 = bf16[16,13,128,128]{3,2,1,0:T(8,128)(2,1)} broadcast(bf16[13,128,128]{2,1,0:T(8,128)(2,1)} %bitcast.109), dimensions={1,2,3} | broadcast | bytes 7241728 | tf_op jit(solution)/shard_map/stack | solution.py:48
  14.2 8.7 %all-to-all-start = ((bf16[16,13,128,128]{3,2,1,0:T(8,128)(2,1)}), bf16[16,13,128,128]{3,2,1,0:T(8,128)(2,1)}, u32[]{:S(2)}, u32[]{:S(2)}) async-start(bf16[16,13,128,128]{3,2,1,0:T(8,128)(2,1)} %stack.14), calls=%async_computation | async-start | bytes 13631488 | tf_op jit(solution)/shard_map/all_to_all | solution.py:48
  23.0 0.1 mul.94
  23.7 0.2 convert_reduce_fusion.1
  23.9 0.2 convert_reduce_fusion.2
  24.1 0.3 select_reduce_fusion.1
  24.4 0.1 reshape.268
  24.6 0.1 add.157
  24.7 0.2 copy.83
  25.0 38.2 %all-gather.4.cloned.1.call-done = bf16[128,8192]{1,0:T(8,128)(2,1)} async-done(((bf16[8,8192]{1,0:T(8,128)(2,1)}), bf16[128,8192]{1,0:T(8,128)(2,1)}) %all-gather.4.cloned.1.call-update) | async-done | bytes 2097168 | tf_op jit(solution)/shard_map/all_gather | solution.py:22
  63.2 4.1 copy.77
  67.3 3.2 copy.79
  70.5 8.3 %gather_fusion = bf16[224,128,128]{2,1,0:T(8,128)(2,1)} fusion(bf16[128,64,128]{2,0,1:T(8,128)(2,1)S(1)} %copy.79, s32[1024]{0:T(1024)S(1)} %pad_clamp_fusion.3), kind=kCustom, calls=%fused_computation.2 | custom fusion | bytes 14680960 | tf_op jit(solution)/shard_map/jit(_take)/gather | solution.py:58
  78.8 12.8 %gather_fusion.1 = bf16[416,128,128]{2,1,0:T(8,128)(2,1)} fusion(bf16[128,64,128]{2,0,1:T(8,128)(2,1)S(1)} %copy.79, s32[1024]{0:T(1024)S(1)} %pad_clamp_fusion.1), kind=kCustom, calls=%fused_computation.3 | custom fusion | bytes 27264640 | tf_op jit(solution)/shard_map/jit(_take)/gather | solution.py:97
  91.6 12.7 %copy.90 = bf16[128,416,128]{2,1,0:T(8,128)(2,1)} copy(bf16[128,416,128]{2,0,1:T(8,128)(2,1)} %bitcast.95) | data formatting | bytes 27262976 | tf_op jit(solution)/shard_map/jit(_take)/gather | solution.py:97
  104.3 3.6 broadcast_select_fusion.2
  108.0 11.5 %broadcast_select_fusion.1 = bf16[128,2,208,128]{3,2,1,0:T(8,128)(2,1)} fusion(bf16[128,2,208,128]{3,2,1,0:T(8,128)(2,1)} %bitcast.93, pred[2,208]{1,0:T(4,128)(4,1)S(1)} %compare_and_fusion.2), kind=kLoop, calls=%fused_computation.10 | loop fusion | flops 6815744 | bytes 27263392 | tf_op jit(solution)/shard_map/jit(_take)/select_n | solution.py:97
  119.5 83.8 %all-gather.6.cloned.1.call-done = bf16[1,208,128,128]{3,2,0,1:T(8,128)(2,1)} async-done(((bf16[1,13,128,128]{3,2,0,1:T(8,128)(2,1)}), bf16[1,208,128,128]{3,2,0,1:T(8,128)(2,1)}) %all-gather.6.cloned.1.call-update) | async-done | bytes 6815760 | tf_op jit(solution)/shard_map/all_gather | solution.py:50
  203.3 5.8 %gather_fusion.4 = bf16[112,128,128]{2,1,0:T(8,128)(2,1)} fusion(bf16[208,128,128]{2,1,0:T(8,128)(2,1)} %bitcast.106, s32[1024]{0:T(1024)S(1)} %pad_clamp_fusion.2), kind=kCustom, calls=%fused_computation.1.clone | custom fusion | bytes 7340480 | tf_op jit(solution)/shard_map/jit(_take)/gather | solution.py:55
  209.1 4.3 broadcast_select_fusion.3
  213.4 6.0 %gather_fusion.3 = bf16[112,128,128]{2,1,0:T(8,128)(2,1)} fusion(bf16[208,128,128]{2,1,0:T(8,128)(2,1)} %bitcast.1, s32[1024]{0:T(1024)S(1)} %pad_clamp_fusion.4), kind=kCustom, calls=%fused_computation.clone | custom fusion | bytes 7340480 | tf_op jit(solution)/shard_map/jit(_take)/gather | solution.py:52
  219.4 2.6 broadcast_select_fusion.4
  222.0 0.5 copy-done.1
  222.5 5.0 fusion.12
  227.5 1.3 fusion.13
  228.8 0.3 fusion.16
  229.1 0.2 copy.84
  229.3 0.2 copy.85
  229.5 10.5 %fusion.8 = f32[2,7,16,128,128]{4,3,2,1,0:T(8,128)} fusion(bf16[1,7,16,128,128]{4,3,2,1,0:T(8,128)(2,1)} %bitcast.98, bf16[1,7,16,128,128]{4,3,2,1,0:T(8,128)(2,1)} %bitcast.101, bf16[128,1,7,128]{3,0,2,1:T(8,128)(2,1)S(1)} %copy.85, bf16[128,1,7,128]{3,0,2,1:T(8,128)(2,1)S(1)} %copy.84), kind=kOutput, calls=%fused_computation.12 | convolution fusion | flops 943423488 | bytes 22478848 | tf_op jit(solution)/shard_map/nmfc,mfkrc->mfknr/dot_general | solution.py:82
  240.0 15.2 %copy.86 = f32[224,128,128]{2,1,0:T(8,128)} copy(f32[224,128,128]{1,2,0:T(8,128)} %bitcast.92) | data formatting | bytes 29360128 | tf_op jit(solution)/shard_map/reshape | solution.py:85
  255.2 2.5 broadcast_in_dim.57
  257.6 46.3 %scatter_fusion = f32[64,128,128]{2,1,0:T(8,128)} fusion(f32[64,128,128]{2,1,0:T(8,128)} %broadcast_in_dim.57, s32[224]{0:T(256)S(1)} %reshape.312, f32[224,128,128]{2,1,0:T(8,128)} %copy.86), kind=kCustom, calls=%fused_computation.5 | custom fusion | flops 3670016 | bytes 44041088 | tf_op jit(solution)/shard_map/scatter-add | solution.py:86
  304.0 2.6 convert_bitcast_fusion
  306.5 3.0 copy.87
  309.6 12.8 %gather_fusion.2 = bf16[416,128,128]{2,1,0:T(8,128)(2,1)} fusion(bf16[128,16,128]{2,0,1:T(8,128)(2,1)S(1)} %bitcast.91, s32[1024]{0:T(1024)S(1)} %pad_clamp_fusion), kind=kCustom, calls=%fused_computation.4 | custom fusion | bytes 27264640 | tf_op jit(solution)/shard_map/jit(_take)/gather | solution.py:100
  322.4 13.1 %copy.91 = bf16[128,416,128]{2,1,0:T(8,128)(2,1)S(1)} copy(bf16[128,416,128]{2,0,1:T(8,128)(2,1)} %bitcast.96) | data formatting | bytes 27262976 | tf_op jit(solution)/shard_map/jit(_take)/gather | solution.py:100
  335.5 5.8 %broadcast_select_fusion = bf16[128,2,208,128]{3,2,1,0:T(8,128)(2,1)} fusion(bf16[128,2,208,128]{3,2,1,0:T(8,128)(2,1)S(1)} %bitcast.94, pred[2,208]{1,0:T(4,128)(4,1)S(1)} %get-tuple-element.28), kind=kLoop, calls=%fused_computation.9 | loop fusion | flops 6815744 | bytes 27263392 | tf_op jit(solution)/shard_map/jit(_take)/select_n | solution.py:100
  341.3 37.7 %fusion.3 = bf16[208,2,128,128]{3,2,1,0:T(8,128)(2,1)} fusion(bf16[128,2,208,128]{3,2,1,0:T(8,128)(2,1)} %broadcast_select_fusion, bf16[128,2,208,128]{3,2,1,0:T(8,128)(2,1)} %broadcast_select_fusion.1), kind=kOutput, calls=%fused_computation.11 | convolution fusion | flops 1751646208 | bytes 40894464 | tf_op jit(solution)/shard_map/nmsr,nmsc->smrc/dot_general | solution.py:104
  379.0 0.6 copy-done.6
  379.7 0.6 dynamic-slice
  380.9 0.8 copy.94
  381.8 29.9 %all-reduce.4.cloned.1.call-done = bf16[128,8192]{0,1:T(8,128)(2,1)} async-done(((bf16[128,8192]{0,1:T(8,128)(2,1)}), bf16[128,8192]{0,1:T(8,128)(2,1)}) %all-reduce.4.cloned.1.call-update) | async-done | bytes 2097168
  411.7 2.2 constant_dynamic-slice_fusion
  413.9 1.4 copy.95
  415.3 83.3 %reduce-scatter.3.cloned.1.call-done = bf16[13,2,128,128]{3,2,1,0:T(8,128)(2,1)} async-done(((bf16[208,2,128,128]{3,2,1,0:T(8,128)(2,1)}), bf16[13,2,128,128]{3,2,1,0:T(8,128)(2,1)}) %reduce-scatter.3.cloned.1.call-update) | async-done | bytes 851984 | tf_op jit(solution)/shard_map/reduce_scatter | solution.py:103
  498.6 2.1 slice_bitcast_fusion.4
  (52 shorter events, 1.0 us)
Async XLA Ops:
  7.2 56.0 %all-gather.4.cloned.1.call-start = ((), (), s32[]{:S(2)}) async-start(), calls=%async_computation.2 | async-start | bytes 2228224 | tf_op jit(solution)/shard_map/all_gather | solution.py:22
  7.9 195.4 %all-gather.6.cloned.1.call-start = ((), (), s32[]{:S(2)}) async-start(), calls=%async_computation.4 | async-start | bytes 7241728 | tf_op jit(solution)/shard_map/all_gather | solution.py:50
  14.2 8.8 %copy-start.4 = (s32[2,7,16]{2,0,1:T(2,128)S(1)}, s32[2,7,16]{2,0,1:T(2,128)}, u32[]{:S(2)}) copy-start(s32[2,7,16]{2,0,1:T(2,128)} %param.12) | copy-start | bytes 2692
  14.2 9.1 %copy-start.5 = (s32[2,7,16]{2,0,1:T(2,128)S(1)}, s32[2,7,16]{2,0,1:T(2,128)}, u32[]{:S(2)}) copy-start(s32[2,7,16]{2,0,1:T(2,128)} %param.13) | copy-start | bytes 2692
  14.2 10.4 %copy-start.3 = (bf16[128,896]{1,0:T(8,128)(2,1)S(1)}, bf16[128,896]{1,0:T(8,128)(2,1)}, u32[]{:S(2)}) copy-start(bf16[128,896]{1,0:T(8,128)(2,1)} %param.9) | copy-start | bytes 688132
  14.2 199.2 %all-to-all-start = ((bf16[16,13,128,128]{3,2,1,0:T(8,128)(2,1)}), bf16[16,13,128,128]{3,2,1,0:T(8,128)(2,1)}, u32[]{:S(2)}, u32[]{:S(2)}) async-start(bf16[16,13,128,128]{3,2,1,0:T(8,128)(2,1)} %stack.14), calls=%async_computation | async-start | bytes 13631488 | tf_op jit(solution)/shard_map/all_to_all | solution.py:48
  23.0 388.7 %all-reduce.4.cloned.1.call-start = ((), (), s32[]{:S(2)}) async-start(), calls=%async_computation.5 | async-start | bytes 4194304
  91.6 12.7 %copy-start = (bf16[224,128,128]{2,1,0:T(8,128)(2,1)S(1)}, bf16[224,128,128]{2,1,0:T(8,128)(2,1)}, u32[]{:S(2)}) copy-start(bf16[224,128,128]{2,1,0:T(8,128)(2,1)} %gather_fusion) | copy-start | bytes 22020100
  213.4 14.1 %slice-start = ((s8[7340032]{0:T(1024)(128)(4,1)}), s8[3145728]{0:T(1024)(128)(4,1)S(1)}, s32[]{:S(2)}) async-start(s8[7340032]{0:T(1024)(128)(4,1)} %bitcast.104), calls=%async_computation.6 | async-start | bytes 6291456
  219.4 3.1 copy-start.1
  219.4 8.1 %slice-start.1 = ((s8[7340032]{0:T(1024)(128)(4,1)}), s8[4194304]{0:T(1024)(128)(4,1)S(1)}, s32[]{:S(2)}) async-start(s8[7340032]{0:T(1024)(128)(4,1)} %bitcast.104), calls=%async_computation.7 | async-start | bytes 8388608
  222.0 6.8 %copy-start.2 = (bf16[112,128,128]{2,1,0:T(8,128)(2,1)}, bf16[112,128,128]{2,1,0:T(8,128)(2,1)S(1)}, u32[]{:S(2)}) copy-start(bf16[112,128,128]{2,1,0:T(8,128)(2,1)S(1)} %broadcast_select_fusion.4) | copy-start | bytes 11010052
  309.5 189.1 %reduce-scatter.3.cloned.1.call-start = ((), (), s32[]{:S(2)}) async-start(), calls=%async_computation.3 | async-start | bytes 14483456 | tf_op jit(solution)/shard_map/reduce_scatter | solution.py:103
  379.0 0.7 copy-start.6
Sparse Core Ops, SparseCore 0:
  10.4 52.7 all-gather.3
  65.0 138.2 all-gather.5
  309.6 101.9 all-reduce.3
  414.1 84.4 reduce-scatter.2
